TPU v7x, 512 devices: a whole 4x8x8 slice. The times are simulated.
512 devices in a mesh: dp: 4 (over y_lo, core), seq: 4 (over x), fsdp: 32 (over y_hi, z).
Axes of the slice: x: 4, y: 8 (y_hi: 4, y_lo: 2; y = y_hi * 2 + y_lo), z: 8, core: 2. Of those that a mesh axis runs over, the one named last changes fastest.
Arguments:
- patches: bfloat16 [128, 768, 6144], P(('dp', 'fsdp'), 'seq'), may hold values from -100 to 100
- segments: int32 [128, 768], P(('dp', 'fsdp'), 'seq'), may hold values from 0 to 7, never falling along the last dimension, each value on 1 to 384 neighbouring positions
- qkv_weight: bfloat16 [6144, 384], P('fsdp'), may hold values from -0.078125 to 0.078125
- cotangent: bfloat16 [128, 768, 128], P(('dp', 'fsdp'), 'seq'), may hold values from -6 to 6
Outputs:
- input_grad: bfloat16 [128, 768, 6144], P(('dp', 'fsdp'), 'seq')
- weight_grad: float32 [6144, 384], P('fsdp')
Inputs may be any that keep to these rules, and one draw needn't show every extreme that they name: `segments`: within a sequence the image number never falls; each of the 8 images has 1 to 384 patches and one has exactly 384.
All inputs are finite; a program needn't handle non-finite values.
Results may differ from a plain program's by a relative error of at most 0.034.
The roundings to bfloat16 on the way count: a program that leaves them out, or rounds other values in their place, can miss the bound.
Values may be sent and summed in bfloat16 or wider, within the bound.
No kernel may reach another device: no remote copies, remote signals or barrier semaphores. Data moves between devices by JAX's collectives and lax.ppermute only.
A program may use at most 64 MiB of HBM per device.

v0:
```python
import functools
import jax
import jax.numpy as jnp
from jax import lax
from jax.sharding import PartitionSpec as P


def contract_first(left, right):
    return lax.dot_general(
        left, right, (((0,), (0,)), ((), ())), preferred_element_type=jnp.float32
    )


def contract_last(left, right):
    return lax.dot_general(
        left, right, (((1,), (1,)), ((), ())), preferred_element_type=jnp.float32
    )


def dp_partner(x, bit):
    pairs = [(i, i ^ bit) for i in range(lax.axis_size("dp"))]
    return lax.ppermute(x, "dp", perm=pairs)


class Ring:

    def __init__(self, axis, size, inner):
        self.axis, self.size, self.inner = (axis, size, inner)

    def total(self):
        return lax.axis_size(self.axis)

    def position(self):
        return lax.axis_index(self.axis) // self.inner % self.size

    def shift(self, x, step):
        n, inner, total = (self.size, self.inner, self.total())
        pairs = []
        for i in range(total):
            pos = i // inner % n
            base = i - pos * inner
            pairs.append((i, base + (pos + step) % n * inner))
        return lax.ppermute(x, self.axis, perm=pairs)


def ring_gather(x, ring, beside=None, late=None):
    n = ring.size
    got, slot = ([x], {0: 0})
    cw, ccw = (x, x)
    last_cw = n - 1 if (n - 1) % 2 == 1 else n - 2
    last_ccw = n - 1 if (n - 1) % 2 == 0 else n - 2
    for t in range(1, n):
        if t % 2 == 1:
            cw = ring.shift(cw, 1)
            if t == 1 and beside is not None:
                cw, beside = lax.optimization_barrier((cw, beside))
            if t == last_cw and late is not None:
                cw, late = lax.optimization_barrier((cw, late))
            slot[(n - (t + 1) // 2) % n] = len(got)
            got.append(cw)
        else:
            ccw = ring.shift(ccw, -1)
            if t == last_ccw and late is not None:
                value, make = late
                ccw, value = lax.optimization_barrier((ccw, value))
                late = make(value)
            slot[t // 2] = len(got)
            got.append(ccw)
    if late is not None:
        return (jnp.stack(got), [slot[k] for k in range(n)], late)
    return (jnp.stack(got), [slot[k] for k in range(n)], beside)


def ring_reduce_scatter(blocks, ring, axis=0, beside=None):
    n = ring.size
    me = ring.position()

    def pick(index):
        return lax.dynamic_index_in_dim(blocks, index % n, axis=axis, keepdims=False)

    total = pick(me)
    if n == 1:
        return (total, beside)
    up, down = (n // 2, (n - 1) // 2)
    acc = pick(me + up)
    for t in range(1, up + 1):
        acc = ring.shift(acc.astype(jnp.bfloat16), 1)
        if t == 1 and beside is not None:
            acc, beside = lax.optimization_barrier((acc, beside))
        acc = acc.astype(jnp.float32)
        if t < up:
            acc = acc + pick(me + up - t)
    total = total + acc
    if down:
        acc = pick(me - down)
        for t in range(1, down + 1):
            acc = ring.shift(acc.astype(jnp.bfloat16), -1).astype(jnp.float32)
            if t < down:
                acc = acc + pick(me - down + t)
        total = total + acc
    return (total, beside)


def shards(patches, segments, qkv_weight, cotangent, inner_fsdp):
    features = patches[0]
    image_ids = segments[0]
    grad_out = cotangent[0]
    width_head = cotangent.shape[2]
    width_all = qkv_weight.shape[1]
    rows_w = qkv_weight.shape[0]
    half = width_all // 2
    scale = width_head ** (-0.5)
    core = lax.axis_index("dp") % 2
    first = core == 0
    outer_fsdp = lax.axis_size("fh")
    n_fsdp = outer_fsdp * inner_fsdp
    ring_y = Ring("fh", outer_fsdp, 1)
    ring_z = Ring("fz", inner_fsdp, 1)
    ring_x = Ring("seq", lax.axis_size("seq"), 1)
    w_mine = lax.dynamic_slice_in_dim(qkv_weight, core * half, half, axis=1)
    stack_y = lax.all_gather(w_mine, "fh", axis=0, tiled=False)
    relayout = lambda f: f.reshape(f.shape[0], outer_fsdp, inner_fsdp, rows_w)
    stack_zy, slot_z, blocked = ring_gather(stack_y, ring_z, late=(features, relayout))
    flat = stack_zy.reshape(-1, rows_w, half)
    me_y, me_z = (ring_y.position(), ring_z.position())
    absolute = jnp.arange(n_fsdp, dtype=jnp.int32)
    rel_z = (absolute % inner_fsdp - me_z) % inner_fsdp
    order = jnp.asarray(slot_z, jnp.int32)[rel_z] * outer_fsdp + absolute // inner_fsdp
    w_mine_all = jnp.take(flat, order, axis=0, mode="clip").reshape(n_fsdp * rows_w, half)
    w_other_all = dp_partner(w_mine_all, 1)
    h_mine = jnp.dot(features, w_mine_all, preferred_element_type=jnp.float32)
    h_other = jnp.dot(features, w_other_all, preferred_element_type=jnp.float32)
    projected = jnp.where(
        first,
        jnp.concatenate([h_mine, h_other], axis=1),
        jnp.concatenate([h_other, h_mine], axis=1),
    )
    heads = projected.astype(jnp.bfloat16)
    n_rows = features.shape[0]
    n_x = ring_x.size
    me_x = ring_x.position()
    ids_col = jnp.broadcast_to(image_ids.astype(jnp.bfloat16)[:, None], (n_rows, width_head))
    packed = jnp.concatenate([heads, grad_out, ids_col], axis=1)
    packed_all = lax.all_gather(packed, "seq", axis=0, tiled=True)
    query_all = packed_all[:, :width_head]
    keys_all = packed_all[:, width_head : 2 * width_head]
    values_all = packed_all[:, 2 * width_head : 3 * width_head]
    grad_out_all = packed_all[:, 3 * width_head : 4 * width_head]
    images_all = packed_all[:, 4 * width_head]
    scores = contract_last(query_all, keys_all) * scale
    allowed = images_all[:, None] == images_all[None, :]
    highest = jnp.max(jnp.where(allowed, scores, -jnp.inf), axis=1)
    summed = jnp.sum(jnp.where(allowed, jnp.exp(scores - highest[:, None]), 0.0), axis=1)
    log_total = highest + jnp.log(summed)
    attention = jnp.where(allowed, jnp.exp(scores - log_total[:, None]), 0.0)
    attention_low = attention.astype(jnp.bfloat16)
    output = jnp.dot(attention_low, values_all, preferred_element_type=jnp.float32)
    delta_rows = jnp.sum(grad_out_all.astype(jnp.float32) * output, axis=1)
    grad_attention = contract_last(grad_out_all, values_all)
    grad_scores = (attention * (grad_attention - delta_rows[:, None]) * scale).astype(jnp.bfloat16)
    start = me_x * n_rows
    own_rows = lax.dynamic_slice_in_dim(grad_scores, start, n_rows, axis=0)
    own_cols = lax.dynamic_slice_in_dim(grad_scores, start, n_rows, axis=1)
    own_attention = lax.dynamic_slice_in_dim(attention_low, start, n_rows, axis=1)
    grad_query = jnp.dot(own_rows, keys_all, preferred_element_type=jnp.float32)
    grad_key = contract_first(own_cols, query_all)
    grad_value = contract_first(own_attention, grad_out_all)
    grad_heads = jnp.concatenate([grad_query, grad_key, grad_value], axis=1).astype(jnp.bfloat16)
    g_lo = grad_heads[:, :half]
    g_hi = grad_heads[:, half:]
    g_mine = jnp.where(first, g_lo, g_hi)
    g_other = jnp.where(first, g_hi, g_lo)
    input_grad = (contract_last(g_mine, w_mine_all) + contract_last(g_other, w_other_all)).astype(
        jnp.bfloat16
    )
    wg_other = jnp.einsum("pyzd,pc->zydc", blocked, g_other, preferred_element_type=jnp.float32)
    wg_from_partner = dp_partner(wg_other.astype(jnp.bfloat16), 1)
    wg_mine = jnp.einsum("pyzd,pc->zydc", blocked, g_mine, preferred_element_type=jnp.float32)
    wg_mine, wg_from_partner = lax.optimization_barrier((wg_mine, wg_from_partner))
    blocks = wg_mine + wg_from_partner.astype(jnp.float32)
    over_z, input_grad = ring_reduce_scatter(blocks, ring_z, axis=0, beside=input_grad)
    over_fsdp, _ = ring_reduce_scatter(over_z, ring_y)
    by_seq = lax.all_gather(over_fsdp, "seq", axis=0, tiled=False)
    over_seq = by_seq[0]
    for s_i in range(1, by_seq.shape[0]):
        over_seq = over_seq + by_seq[s_i]
    by_dp = lax.all_gather(over_seq, "dp", axis=0, tiled=False)
    halves = []
    for c in range(2):
        part = by_dp[c]
        for d in range(c + 2, by_dp.shape[0], 2):
            part = part + by_dp[d]
        halves.append(part)
    weight_grad = jnp.concatenate(halves, axis=1)
    return (input_grad[None], weight_grad)


def inner_ring_size(mesh):
    axis = mesh.axis_names.index("fsdp")
    line = mesh.devices[tuple((0 if a != axis else slice(None) for a in range(mesh.devices.ndim)))]
    line = list(line)
    if not hasattr(line[0], "coords"):
        return len(line)
    count = 1
    while count < len(line) and line[count].coords[1] == line[0].coords[1]:
        count += 1
    return count


def solution(mesh):
    inner = inner_ring_size(mesh)
    sizes = dict(zip(mesh.axis_names, mesh.devices.shape))
    split = jax.sharding.Mesh(
        mesh.devices.reshape(sizes["dp"], sizes["seq"], sizes["fsdp"] // inner, inner),
        ("dp", "seq", "fh", "fz"),
    )
    rows = ("dp", "fh", "fz")
    placed = (P(rows, "seq", None), P(rows, "seq"), P(("fh", "fz"), None), P(rows, "seq", None))
    return jax.shard_map(
        functools.partial(shards, inner_fsdp=inner),
        mesh=split,
        in_specs=placed,
        out_specs=(P(rows, "seq", None), P(("fh", "fz"), None)),
        check_vma=False,
    )
```

profile of v0, /device:TPU:75, one launch (start us, length us, event | category | flops | bytes accessed | tf_op | source)
XLA Modules:
  0.0 222.7 jit_solution(9267431359710863556)
XLA Ops:
  1.6 13.7 %all-gather = bf16[768,192]{1,0:T(8,128)(2,1)S(1)} all-gather(bf16[192,192]{1,0:T(8,128)(2,1)S(1)} %constant_dynamic-slice_fusion), channel_id=2, replica_groups=mesh['dp'=4,'seq'=4,'fh'=4,'fz'=8] {'fh'}, dimensions={0}, use_global_device_ids=true | all-gather | bytes 368640 | tf_op jit(solution)/shard_map/all_gather | solution.py:121
  15.3 4.0 %collective-permute-start = (bf16[4,192,192]{2,1,0:T(8,128)(2,1)S(1)}, bf16[4,192,192]{2,1,0:T(8,128)(2,1)}, u32[]{:S(2)}, u32[]{:S(2)}) collective-permute-start(bf16[4,192,192]{2,1,0:T(8,128)(2,1)S(1)} %bitcast.108), channel_id=1, source_target_pairs={{0,1},{1,2},{2,3},{3,4},{4,5},{5,6},{6,7},{7,0},{8,9},{9,10},{10,1... | collective-permute-start | bytes 884744 | tf_op jit(solution)/shard_map/ppermute | solution.py:43
  19.3 1.9 collective-permute-start.1
  22.1 1.5 gather_fusion
  24.0 4.0 %collective-permute-start.2 = (bf16[4,192,192]{2,1,0:T(8,128)(2,1)}, bf16[4,192,192]{2,1,0:T(8,128)(2,1)S(1)}, u32[]{:S(2)}, u32[]{:S(2)}) collective-permute-start(bf16[4,192,192]{2,1,0:T(8,128)(2,1)} %collective-permute-done), channel_id=1, source_target_pairs={{0,1},{1,2},{2,3},{3,4},{4,5},{5,6},{6,7},{7,0},{8,9},{9,10},{10,1... | collective-permute-start | bytes 884744 | tf_op jit(solution)/shard_map/ppermute | solution.py:43
  28.0 1.8 bitcast_dynamic-update-slice_fusion.6
  29.8 6.4 %collective-permute-start.3 = (bf16[4,192,192]{2,1,0:T(8,128)(2,1)S(1)}, bf16[4,192,192]{2,1,0:T(8,128)(2,1)S(1)}, u32[]{:S(2)}, u32[]{:S(2)}) collective-permute-start(bf16[4,192,192]{2,1,0:T(8,128)(2,1)S(1)} %collective-permute-done.1), channel_id=1, source_target_pairs={{0,7},{1,0},{2,1},{3,2},{4,3},{5,4},{6,5},{7,6},{8,15},{9,8},{10,9... | collective-permute-start | bytes 884744 | tf_op jit(solution)/shard_map/ppermute | solution.py:43
  37.9 1.9 collective-permute-start.4
  40.9 4.6 %collective-permute-start.5 = (bf16[4,192,192]{2,1,0:T(8,128)(2,1)S(1)}, bf16[4,192,192]{2,1,0:T(8,128)(2,1)S(1)}, u32[]{:S(2)}, u32[]{:S(2)}) collective-permute-start(bf16[4,192,192]{2,1,0:T(8,128)(2,1)S(1)} %collective-permute-done.3), channel_id=1, source_target_pairs={{0,7},{1,0},{2,1},{3,2},{4,3},{5,4},{6,5},{7,6},{8,15},{9,8},{10,9... | collective-permute-start | bytes 884744 | tf_op jit(solution)/shard_map/ppermute | solution.py:43
  46.3 1.4 collective-permute-done.4
  47.7 1.9 collective-permute-start.6
  49.6 1.8 bitcast_dynamic-update-slice_fusion.2
  51.5 4.5 %reshape.141 = bf16[192,4,8,192]{3,2,1,0:T(8,128)(2,1)} reshape(bf16[192,6144]{1,0:T(8,128)(2,1)S(1)} %bitcast.105) | data formatting | bytes 4718592 | tf_op jit(solution)/shard_map/reshape | solution.py:122
  56.8 1.4 collective-permute-done.6
  58.2 1.8 bitcast_dynamic-update-slice_fusion
  60.0 2.6 %gather_fusion.1 = bf16[32,192,192]{2,1,0:T(8,128)(2,1)S(1)} fusion(bf16[32,192,192]{2,1,0:T(8,128)(2,1)} %bitcast.106, s32[1024]{0:T(1024)S(1)} %pad_clamp_fusion), kind=kCustom, calls=%fused_computation.1 | custom fusion | bytes 4718720 | tf_op jit(solution)/shard_map/jit(_take)/gather | solution.py:129
  62.6 2.6 %copy.31 = bf16[6144,192]{0,1:T(8,128)(2,1)} copy(bf16[6144,192]{1,0:T(8,128)(2,1)S(1)} %bitcast.102) | data formatting | bytes 4718592 | tf_op jit(solution)/shard_map/reshape | solution.py:129
  65.2 10.2 %collective-permute-start.7 = (bf16[6144,192]{0,1:T(8,128)(2,1)}, bf16[6144,192]{0,1:T(8,128)(2,1)}, u32[]{:S(2)}, u32[]{:S(2)}) collective-permute-start(bf16[6144,192]{0,1:T(8,128)(2,1)} %copy.31), channel_id=1, source_target_pairs={{0,128},{128,0},{256,384},{384,256},{1,129},{129,1},{257,385},{385... | collective-permute-start | bytes 7077896 | tf_op jit(solution)/shard_map/ppermute | solution.py:22
  75.5 2.6 %convolution_bitcast_fusion.1 = bf16[192,192]{1,0:T(8,128)(2,1)S(1)} fusion(bf16[6144,192]{1,0:T(8,128)(2,1)S(1)} %bitcast.103, bf16[1,192,6144]{2,1,0:T(8,128)(2,1)} %param.5), kind=kOutput, calls=%fused_computation.21 | convolution fusion | flops 452984832 | bytes 4792320 | tf_op jit(solution)/shard_map/dot_general | solution.py:131
  78.1 1.8 collective-permute-done.7
  79.9 2.5 %convolution_bitcast_fusion = bf16[192,192]{1,0:T(8,128)(2,1)S(1)} fusion(bf16[6144,192]{0,1:T(8,128)(2,1)} %collective-permute-done.7, bf16[1,192,6144]{2,1,0:T(8,128)(2,1)S(1)} %copy-done.5), kind=kOutput, calls=%fused_computation.20 | convolution fusion | flops 452984832 | bytes 4792320 | tf_op jit(solution)/shard_map/dot_general | solution.py:132
  82.7 12.4 %all_gather.21 = bf16[768,640]{1,0:T(8,128)(2,1)S(1)} all-gather(bf16[192,640]{1,0:T(8,128)(2,1)S(1)} %pad_maximum_fusion.1), channel_id=1, replica_groups=mesh['dp'=4,'seq'=4,'fh'=4,'fz'=8] {'seq'}, dimensions={0}, use_global_device_ids=true | all-gather | bytes 1228800 | tf_op jit(solution)/shard_map/all_gather | solution.py:144
  99.5 4.1 %convert_bitcast_fusion = bf16[8,4,192,192]{2,3,0,1:T(8,128)(2,1)} fusion(bf16[192,4,8,192]{3,2,1,0:T(8,128)(2,1)S(1)} %copy-done.1, pred[]{:T(512)S(6)} %eq.39, bf16[192,128]{1,0:T(8,128)(2,1)S(1)} %convolution_convert_fusion.1, bf16[192,128]{1,0:T(8,128)(2,1)S(1)} %convolution_convert_fusion.2, bf16[192,128]{1,0:T(8,128)(2,1)S(1)} %convolution_convert_fusion), kind=kOutput, calls=%fused_computation.8 | convolution fusion | flops 454496256 | bytes 4866049 | tf_op jit(solution)/shard_map/pyzd,pc->zydc/dot_general | solution.py:176
  103.6 5.4 %collective-permute-start.8 = (bf16[8,4,192,192]{2,3,0,1:T(8,128)(2,1)}, bf16[8,4,192,192]{2,3,0,1:T(8,128)(2,1)}, u32[]{:S(2)}, u32[]{:S(2)}) collective-permute-start(bf16[8,4,192,192]{2,3,0,1:T(8,128)(2,1)} %convert_bitcast_fusion), channel_id=1, source_target_pairs={{0,128},{128,0},{256,384},{384,256},{1,129},{129,1},{257,385},{385... | collective-permute-start | bytes 7077896 | tf_op jit(solution)/shard_map/ppermute | solution.py:22
  111.0 2.4 %fusion.5 = f32[8,4,192,192]{2,3,0,1:T(8,128)S(1)} fusion(bf16[192,4,8,192]{3,2,1,0:T(8,128)(2,1)S(1)} %copy-done.2, pred[]{:T(512)S(6)} %eq.39, bf16[192,128]{1,0:T(8,128)(2,1)S(1)} %convolution_convert_fusion.1, bf16[192,128]{1,0:T(8,128)(2,1)S(1)} %convolution_convert_fusion.2, bf16[192,128]{1,0:T(8,128)(2,1)S(1)} %convolution_convert_fusion), kind=kOutput, calls=%fused_computation.13 | convolution fusion | flops 453316608 | bytes 7225345 | tf_op jit(solution)/shard_map/pyzd,pc->zydc/dot_general | solution.py:178
  114.5 3.0 %convert_add_fusion = f32[8,4,192,192]{2,3,0,1:T(8,128)S(1)} fusion(f32[8,4,192,192]{2,3,0,1:T(8,128)S(1)} %fusion.5, bf16[8,4,192,192]{2,3,0,1:T(8,128)(2,1)} %collective-permute-done.8), kind=kLoop, calls=%fused_computation.4 | loop fusion | flops 2359296 | bytes 11796480 | tf_op jit(solution)/shard_map/add | solution.py:180
  117.6 2.1 collective-permute-start.9
  119.7 3.9 %fusion = bf16[192,6144]{1,0:T(8,128)(2,1)} fusion(f32[192,6144]{1,0:T(8,128)S(1)} %fusion.54, bf16[6144,192]{0,1:T(8,128)(2,1)} %collective-permute-done.7, pred[]{:T(512)S(6)} %eq.39, bf16[192,128]{1,0:T(8,128)(2,1)S(1)} %convolution_convert_fusion.1, bf16[192,128]{1,0:T(8,128)(2,1)S(1)} %convolution_convert_fusion.2, ...), kind=kOutput, calls=%fused_computation.3 | convolution fusion | flops 455675904 | bytes 9584641 | tf_op jit(solution)/shard_map/dot_general | solution.py:15
  123.6 4.7 %collective-permute-start.13 = (bf16[4,192,192]{1,2,0:T(8,128)(2,1)S(1)}, bf16[4,192,192]{1,2,0:T(8,128)(2,1)S(1)}, u32[]{:S(2)}, u32[]{:S(2)}) collective-permute-start(bf16[4,192,192]{1,2,0:T(8,128)(2,1)S(1)} %get-tuple-element.26), channel_id=1, source_target_pairs={{0,7},{1,0},{2,1},{3,2},{4,3},{5,4},{6,5},{7,6},{8,15},{9,8},{10,9... | collective-permute-start | bytes 884744 | tf_op jit(solution)/shard_map/ppermute | solution.py:43
  128.4 3.3 %collective-permute-done.9 = bf16[4,192,192]{1,2,0:T(8,128)(2,1)S(1)} collective-permute-done((bf16[4,192,192]{1,2,0:T(8,128)(2,1)S(1)}, bf16[4,192,192]{1,2,0:T(8,128)(2,1)S(1)}, u32[]{:S(2)}, u32[]{:S(2)}) %collective-permute-start.9) | collective-permute-done | bytes 294944 | tf_op jit(solution)/shard_map/ppermute | solution.py:43
  131.8 1.9 collective-permute-start.10
  133.7 4.2 %collective-permute-done.13 = bf16[4,192,192]{1,2,0:T(8,128)(2,1)S(1)} collective-permute-done((bf16[4,192,192]{1,2,0:T(8,128)(2,1)S(1)}, bf16[4,192,192]{1,2,0:T(8,128)(2,1)S(1)}, u32[]{:S(2)}, u32[]{:S(2)}) %collective-permute-start.13) | collective-permute-done | bytes 294944 | tf_op jit(solution)/shard_map/ppermute | solution.py:43
  137.9 6.4 %collective-permute-done.10 = bf16[4,192,192]{1,2,0:T(8,128)(2,1)S(1)} collective-permute-done((bf16[4,192,192]{1,2,0:T(8,128)(2,1)S(1)}, bf16[4,192,192]{1,2,0:T(8,128)(2,1)S(1)}, u32[]{:S(2)}, u32[]{:S(2)}) %collective-permute-start.10) | collective-permute-done | bytes 294944 | tf_op jit(solution)/shard_map/ppermute | solution.py:43
  144.3 1.6 fusion.17
  145.8 1.9 collective-permute-start.11
  147.7 4.3 %collective-permute-start.14 = (bf16[4,192,192]{1,2,0:T(8,128)(2,1)S(1)}, bf16[4,192,192]{1,2,0:T(8,128)(2,1)S(1)}, u32[]{:S(2)}, u32[]{:S(2)}) collective-permute-start(bf16[4,192,192]{1,2,0:T(8,128)(2,1)S(1)} %get-tuple-element.25), channel_id=1, source_target_pairs={{0,7},{1,0},{2,1},{3,2},{4,3},{5,4},{6,5},{7,6},{8,15},{9,8},{10,9... | collective-permute-start | bytes 884744 | tf_op jit(solution)/shard_map/ppermute | solution.py:43
  152.1 5.3 %collective-permute-done.11 = bf16[4,192,192]{1,2,0:T(8,128)(2,1)S(1)} collective-permute-done((bf16[4,192,192]{1,2,0:T(8,128)(2,1)S(1)}, bf16[4,192,192]{1,2,0:T(8,128)(2,1)S(1)}, u32[]{:S(2)}, u32[]{:S(2)}) %collective-permute-start.11) | collective-permute-done | bytes 294944 | tf_op jit(solution)/shard_map/ppermute | solution.py:43
  158.3 1.6 fusion.16
  159.8 5.2 %collective-permute-start.12 = (bf16[4,192,192]{1,2,0:T(8,128)(2,1)S(1)}, bf16[4,192,192]{1,2,0:T(8,128)(2,1)S(1)}, u32[]{:S(2)}, u32[]{:S(2)}) collective-permute-start(bf16[4,192,192]{1,2,0:T(8,128)(2,1)S(1)} %get-tuple-element.22), channel_id=1, source_target_pairs={{0,1},{1,2},{2,3},{3,4},{4,5},{5,6},{6,7},{7,0},{8,9},{9,10},{10,1... | collective-permute-start | bytes 884744 | tf_op jit(solution)/shard_map/ppermute | solution.py:43
  165.1 1.9 collective-permute-start.15
  167.1 3.3 %collective-permute-done.12 = bf16[4,192,192]{1,2,0:T(8,128)(2,1)S(1)} collective-permute-done((bf16[4,192,192]{1,2,0:T(8,128)(2,1)S(1)}, bf16[4,192,192]{1,2,0:T(8,128)(2,1)S(1)}, u32[]{:S(2)}, u32[]{:S(2)}) %collective-permute-start.12) | collective-permute-done | bytes 294944 | tf_op jit(solution)/shard_map/ppermute | solution.py:43
  170.4 4.8 %collective-permute-done.15 = bf16[4,192,192]{1,2,0:T(8,128)(2,1)S(1)} collective-permute-done((bf16[4,192,192]{1,2,0:T(8,128)(2,1)S(1)}, bf16[4,192,192]{1,2,0:T(8,128)(2,1)S(1)}, u32[]{:S(2)}, u32[]{:S(2)}) %collective-permute-start.15) | collective-permute-done | bytes 294944 | tf_op jit(solution)/shard_map/ppermute | solution.py:43
  176.5 2.7 %collective-permute-start.16 = (bf16[192,192]{0,1:T(8,128)(2,1)S(1)}, bf16[192,192]{0,1:T(8,128)(2,1)S(1)}, u32[]{:S(2)}, u32[]{:S(2)}) collective-permute-start(bf16[192,192]{0,1:T(8,128)(2,1)S(1)} %get-tuple-element.30), channel_id=1, source_target_pairs={{0,8},{8,16},{16,24},{24,0},{1,9},{9,17},{17,25},{25,1},{2,10},{10... | collective-permute-start | bytes 221192 | tf_op jit(solution)/shard_map/ppermute | solution.py:43
  179.3 4.7 %collective-permute-start.18 = (bf16[192,192]{0,1:T(8,128)(2,1)S(1)}, bf16[192,192]{0,1:T(8,128)(2,1)S(1)}, u32[]{:S(2)}, u32[]{:S(2)}) collective-permute-start(bf16[192,192]{0,1:T(8,128)(2,1)S(1)} %get-tuple-element.31), channel_id=1, source_target_pairs={{0,24},{8,0},{16,8},{24,16},{1,25},{9,1},{17,9},{25,17},{2,26},{10... | collective-permute-start | bytes 221192 | tf_op jit(solution)/shard_map/ppermute | solution.py:43
  184.0 1.9 collective-permute-start.17
  186.5 5.4 %collective-permute-done.17 = bf16[192,192]{0,1:T(8,128)(2,1)S(1)} collective-permute-done((bf16[192,192]{0,1:T(8,128)(2,1)S(1)}, bf16[192,192]{0,1:T(8,128)(2,1)S(1)}, u32[]{:S(2)}, u32[]{:S(2)}) %collective-permute-start.17) | collective-permute-done | bytes 73760 | tf_op jit(solution)/shard_map/ppermute | solution.py:43
  192.1 11.0 %all-gather.1 = f32[768,192]{1,0:T(8,128)S(1)} all-gather(f32[192,192]{1,0:T(8,128)S(1)} %copy.39), channel_id=3, replica_groups=mesh['dp'=4,'seq'=4,'fh'=4,'fz'=8] {'seq'}, dimensions={0}, use_global_device_ids=true | all-gather | bytes 737280 | tf_op jit(solution)/shard_map/all_gather | solution.py:183
  203.1 18.7 %all_gather.24 = f32[4,192,192]{2,1,0:T(8,128)S(1)} all-gather(f32[1,192,192]{2,1,0:T(8,128)S(1)} %fusion.28), channel_id=1, replica_groups=mesh['dp'=4,'seq'=4,'fh'=4,'fz'=8] {'dp'}, dimensions={0}, use_global_device_ids=true | all-gather | bytes 737280 | tf_op jit(solution)/shard_map/all_gather | solution.py:187
  (60 shorter events, 18.3 us)
Async XLA Ops:
  0.6 0.9 copy-start
  15.3 8.7 %collective-permute-start = (bf16[4,192,192]{2,1,0:T(8,128)(2,1)S(1)}, bf16[4,192,192]{2,1,0:T(8,128)(2,1)}, u32[]{:S(2)}, u32[]{:S(2)}) collective-permute-start(bf16[4,192,192]{2,1,0:T(8,128)(2,1)S(1)} %bitcast.108), channel_id=1, source_target_pairs={{0,1},{1,2},{2,3},{3,4},{4,5},{5,6},{6,7},{7,0},{8,9},{9,10},{10,1... | collective-permute-start | bytes 884744 | tf_op jit(solution)/shard_map/ppermute | solution.py:43
  19.3 10.5 %collective-permute-start.1 = (bf16[4,192,192]{2,1,0:T(8,128)(2,1)S(1)}, bf16[4,192,192]{2,1,0:T(8,128)(2,1)S(1)}, u32[]{:S(2)}, u32[]{:S(2)}) collective-permute-start(bf16[4,192,192]{2,1,0:T(8,128)(2,1)S(1)} %bitcast.109), channel_id=1, source_target_pairs={{0,7},{1,0},{2,1},{3,2},{4,3},{5,4},{6,5},{7,6},{8,15},{9,8},{10,9... | collective-permute-start | bytes 884744 | tf_op jit(solution)/shard_map/ppermute | solution.py:43
  22.1 29.4 %copy-start.4 = (bf16[1,192,6144]{2,1,0:T(8,128)(2,1)S(1)}, bf16[1,192,6144]{2,1,0:T(8,128)(2,1)}, u32[]{:S(2)}) copy-start(bf16[1,192,6144]{2,1,0:T(8,128)(2,1)} %param.5) | copy-start | bytes 7077892
  24.0 13.9 %collective-permute-start.2 = (bf16[4,192,192]{2,1,0:T(8,128)(2,1)}, bf16[4,192,192]{2,1,0:T(8,128)(2,1)S(1)}, u32[]{:S(2)}, u32[]{:S(2)}) collective-permute-start(bf16[4,192,192]{2,1,0:T(8,128)(2,1)} %collective-permute-done), channel_id=1, source_target_pairs={{0,1},{1,2},{2,3},{3,4},{4,5},{5,6},{6,7},{7,0},{8,9},{9,10},{10,1... | collective-permute-start | bytes 884744 | tf_op jit(solution)/shard_map/ppermute | solution.py:43
  29.8 11.1 %collective-permute-start.3 = (bf16[4,192,192]{2,1,0:T(8,128)(2,1)S(1)}, bf16[4,192,192]{2,1,0:T(8,128)(2,1)S(1)}, u32[]{:S(2)}, u32[]{:S(2)}) collective-permute-start(bf16[4,192,192]{2,1,0:T(8,128)(2,1)S(1)} %collective-permute-done.1), channel_id=1, source_target_pairs={{0,7},{1,0},{2,1},{3,2},{4,3},{5,4},{6,5},{7,6},{8,15},{9,8},{10,9... | collective-permute-start | bytes 884744 | tf_op jit(solution)/shard_map/ppermute | solution.py:43
  37.9 9.8 %collective-permute-start.4 = (bf16[4,192,192]{2,1,0:T(8,128)(2,1)S(1)}, bf16[4,192,192]{2,1,0:T(8,128)(2,1)}, u32[]{:S(2)}, u32[]{:S(2)}) collective-permute-start(bf16[4,192,192]{2,1,0:T(8,128)(2,1)S(1)} %collective-permute-done.2), channel_id=1, source_target_pairs={{0,1},{1,2},{2,3},{3,4},{4,5},{5,6},{6,7},{7,0},{8,9},{9,10},{10,1... | collective-permute-start | bytes 884744 | tf_op jit(solution)/shard_map/ppermute | solution.py:43
  40.9 10.5 %collective-permute-start.5 = (bf16[4,192,192]{2,1,0:T(8,128)(2,1)S(1)}, bf16[4,192,192]{2,1,0:T(8,128)(2,1)S(1)}, u32[]{:S(2)}, u32[]{:S(2)}) collective-permute-start(bf16[4,192,192]{2,1,0:T(8,128)(2,1)S(1)} %collective-permute-done.3), channel_id=1, source_target_pairs={{0,7},{1,0},{2,1},{3,2},{4,3},{5,4},{6,5},{7,6},{8,15},{9,8},{10,9... | collective-permute-start | bytes 884744 | tf_op jit(solution)/shard_map/ppermute | solution.py:43
  47.7 10.5 %collective-permute-start.6 = (bf16[4,192,192]{2,1,0:T(8,128)(2,1)}, bf16[4,192,192]{2,1,0:T(8,128)(2,1)}, u32[]{:S(2)}, u32[]{:S(2)}) collective-permute-start(bf16[4,192,192]{2,1,0:T(8,128)(2,1)} %collective-permute-done.4), channel_id=1, source_target_pairs={{0,1},{1,2},{2,3},{3,4},{4,5},{5,6},{6,7},{7,0},{8,9},{9,10},{10,1... | collective-permute-start | bytes 884744 | tf_op jit(solution)/shard_map/ppermute | solution.py:43
  62.6 12.8 %copy-start.7 = (s32[1,192]{1,0:T(1,128)S(1)}, s32[1,192]{1,0:T(1,128)}, u32[]{:S(2)}) copy-start(s32[1,192]{1,0:T(1,128)} %param.6) | copy-start | bytes 2308
  65.2 14.7 %collective-permute-start.7 = (bf16[6144,192]{0,1:T(8,128)(2,1)}, bf16[6144,192]{0,1:T(8,128)(2,1)}, u32[]{:S(2)}, u32[]{:S(2)}) collective-permute-start(bf16[6144,192]{0,1:T(8,128)(2,1)} %copy.31), channel_id=1, source_target_pairs={{0,128},{128,0},{256,384},{384,256},{1,129},{129,1},{257,385},{385... | collective-permute-start | bytes 7077896 | tf_op jit(solution)/shard_map/ppermute | solution.py:22
  75.5 4.4 %copy-start.5 = (bf16[1,192,6144]{2,1,0:T(8,128)(2,1)S(1)}, bf16[1,192,6144]{2,1,0:T(8,128)(2,1)}, u32[]{:S(2)}) copy-start(bf16[1,192,6144]{2,1,0:T(8,128)(2,1)} %param.5) | copy-start | bytes 7077892
  78.1 4.5 %copy-start.6 = (bf16[1,192,128]{2,1,0:T(8,128)(2,1)S(1)}, bf16[1,192,128]{2,1,0:T(8,128)(2,1)}, u32[]{:S(2)}) copy-start(bf16[1,192,128]{2,1,0:T(8,128)(2,1)} %param.8) | copy-start | bytes 147460
  97.6 1.9 copy-start.1
  103.6 10.9 %collective-permute-start.8 = (bf16[8,4,192,192]{2,3,0,1:T(8,128)(2,1)}, bf16[8,4,192,192]{2,3,0,1:T(8,128)(2,1)}, u32[]{:S(2)}, u32[]{:S(2)}) collective-permute-start(bf16[8,4,192,192]{2,3,0,1:T(8,128)(2,1)} %convert_bitcast_fusion), channel_id=1, source_target_pairs={{0,128},{128,0},{256,384},{384,256},{1,129},{129,1},{257,385},{385... | collective-permute-start | bytes 7077896 | tf_op jit(solution)/shard_map/ppermute | solution.py:22
  109.1 1.9 copy-start.2
  117.5 14.1 %copy-start.3 = (f32[8,4,192,192]{2,3,0,1:T(8,128)}, f32[8,4,192,192]{2,3,0,1:T(8,128)S(1)}, u32[]{:S(2)}) copy-start(f32[8,4,192,192]{2,3,0,1:T(8,128)S(1)} %convert_add_fusion) | copy-start | bytes 14155780
  117.6 14.0 %collective-permute-start.9 = (bf16[4,192,192]{1,2,0:T(8,128)(2,1)S(1)}, bf16[4,192,192]{1,2,0:T(8,128)(2,1)S(1)}, u32[]{:S(2)}, u32[]{:S(2)}) collective-permute-start(bf16[4,192,192]{1,2,0:T(8,128)(2,1)S(1)} %get-tuple-element.27), channel_id=1, source_target_pairs={{0,1},{1,2},{2,3},{3,4},{4,5},{5,6},{6,7},{7,0},{8,9},{9,10},{10,1... | collective-permute-start | bytes 884744 | tf_op jit(solution)/shard_map/ppermute | solution.py:43
  123.6 14.3 %collective-permute-start.13 = (bf16[4,192,192]{1,2,0:T(8,128)(2,1)S(1)}, bf16[4,192,192]{1,2,0:T(8,128)(2,1)S(1)}, u32[]{:S(2)}, u32[]{:S(2)}) collective-permute-start(bf16[4,192,192]{1,2,0:T(8,128)(2,1)S(1)} %get-tuple-element.26), channel_id=1, source_target_pairs={{0,7},{1,0},{2,1},{3,2},{4,3},{5,4},{6,5},{7,6},{8,15},{9,8},{10,9... | collective-permute-start | bytes 884744 | tf_op jit(solution)/shard_map/ppermute | solution.py:43
  131.8 12.5 %collective-permute-start.10 = (bf16[4,192,192]{1,2,0:T(8,128)(2,1)S(1)}, bf16[4,192,192]{1,2,0:T(8,128)(2,1)S(1)}, u32[]{:S(2)}, u32[]{:S(2)}) collective-permute-start(bf16[4,192,192]{1,2,0:T(8,128)(2,1)S(1)} %fusion.18), channel_id=1, source_target_pairs={{0,1},{1,2},{2,3},{3,4},{4,5},{5,6},{6,7},{7,0},{8,9},{9,10},{10,1... | collective-permute-start | bytes 884744 | tf_op jit(solution)/shard_map/ppermute | solution.py:43
  145.8 11.6 %collective-permute-start.11 = (bf16[4,192,192]{1,2,0:T(8,128)(2,1)S(1)}, bf16[4,192,192]{1,2,0:T(8,128)(2,1)S(1)}, u32[]{:S(2)}, u32[]{:S(2)}) collective-permute-start(bf16[4,192,192]{1,2,0:T(8,128)(2,1)S(1)} %get-tuple-element.24), channel_id=1, source_target_pairs={{0,1},{1,2},{2,3},{3,4},{4,5},{5,6},{6,7},{7,0},{8,9},{9,10},{10,1... | collective-permute-start | bytes 884744 | tf_op jit(solution)/shard_map/ppermute | solution.py:43
  147.7 10.5 %collective-permute-start.14 = (bf16[4,192,192]{1,2,0:T(8,128)(2,1)S(1)}, bf16[4,192,192]{1,2,0:T(8,128)(2,1)S(1)}, u32[]{:S(2)}, u32[]{:S(2)}) collective-permute-start(bf16[4,192,192]{1,2,0:T(8,128)(2,1)S(1)} %get-tuple-element.25), channel_id=1, source_target_pairs={{0,7},{1,0},{2,1},{3,2},{4,3},{5,4},{6,5},{7,6},{8,15},{9,8},{10,9... | collective-permute-start | bytes 884744 | tf_op jit(solution)/shard_map/ppermute | solution.py:43
  159.8 10.6 %collective-permute-start.12 = (bf16[4,192,192]{1,2,0:T(8,128)(2,1)S(1)}, bf16[4,192,192]{1,2,0:T(8,128)(2,1)S(1)}, u32[]{:S(2)}, u32[]{:S(2)}) collective-permute-start(bf16[4,192,192]{1,2,0:T(8,128)(2,1)S(1)} %get-tuple-element.22), channel_id=1, source_target_pairs={{0,1},{1,2},{2,3},{3,4},{4,5},{5,6},{6,7},{7,0},{8,9},{9,10},{10,1... | collective-permute-start | bytes 884744 | tf_op jit(solution)/shard_map/ppermute | solution.py:43
  165.1 10.1 %collective-permute-start.15 = (bf16[4,192,192]{1,2,0:T(8,128)(2,1)S(1)}, bf16[4,192,192]{1,2,0:T(8,128)(2,1)S(1)}, u32[]{:S(2)}, u32[]{:S(2)}) collective-permute-start(bf16[4,192,192]{1,2,0:T(8,128)(2,1)S(1)} %get-tuple-element.23), channel_id=1, source_target_pairs={{0,7},{1,0},{2,1},{3,2},{4,3},{5,4},{6,5},{7,6},{8,15},{9,8},{10,9... | collective-permute-start | bytes 884744 | tf_op jit(solution)/shard_map/ppermute | solution.py:43
  176.5 7.5 %collective-permute-start.16 = (bf16[192,192]{0,1:T(8,128)(2,1)S(1)}, bf16[192,192]{0,1:T(8,128)(2,1)S(1)}, u32[]{:S(2)}, u32[]{:S(2)}) collective-permute-start(bf16[192,192]{0,1:T(8,128)(2,1)S(1)} %get-tuple-element.30), channel_id=1, source_target_pairs={{0,8},{8,16},{16,24},{24,0},{1,9},{9,17},{17,25},{25,1},{2,10},{10... | collective-permute-start | bytes 221192 | tf_op jit(solution)/shard_map/ppermute | solution.py:43
  179.3 7.2 %collective-permute-start.18 = (bf16[192,192]{0,1:T(8,128)(2,1)S(1)}, bf16[192,192]{0,1:T(8,128)(2,1)S(1)}, u32[]{:S(2)}, u32[]{:S(2)}) collective-permute-start(bf16[192,192]{0,1:T(8,128)(2,1)S(1)} %get-tuple-element.31), channel_id=1, source_target_pairs={{0,24},{8,0},{16,8},{24,16},{1,25},{9,1},{17,9},{25,17},{2,26},{10... | collective-permute-start | bytes 221192 | tf_op jit(solution)/shard_map/ppermute | solution.py:43
  184.0 7.9 %collective-permute-start.17 = (bf16[192,192]{0,1:T(8,128)(2,1)S(1)}, bf16[192,192]{0,1:T(8,128)(2,1)S(1)}, u32[]{:S(2)}, u32[]{:S(2)}) collective-permute-start(bf16[192,192]{0,1:T(8,128)(2,1)S(1)} %fusion.29), channel_id=1, source_target_pairs={{0,8},{8,16},{16,24},{24,0},{1,9},{9,17},{17,25},{25,1},{2,10},{10... | collective-permute-start | bytes 221192 | tf_op jit(solution)/shard_map/ppermute | solution.py:43
where the time goes:
time: 224 us; the launch traced here: 223 us
  starting transfers between devices  71.7 us (32%)
  blocking collectives  55.8 us (25%)
  waiting for transfers between devices  41.5 us (19%)
  local copies, waits for them, and re-layouts  23.1 us (10%)
  matrix products  19.5 us (9%)
  other arithmetic  9.77 us (4%)
    ppermute x17, starting transfers between devices, shift(): return lax.ppermute(x, self.axis, perm=pairs)  56.1 us
    ppermute x17, waiting for transfers between devices, shift(): return lax.ppermute(x, self.axis, perm=pairs)  38.6 us
    all_gather x1, blocking collectives, shards(): by_dp = lax.all_gather(over_seq, 'dp', axis=0, tiled=False)  18.7 us
    ppermute x2, starting transfers between devices, dp_partner(): return lax.ppermute(x, 'dp', perm=pairs)  15.6 us
    all_gather x1, blocking collectives, shards(): stack_y = lax.all_gather(w_mine, 'fh', axis=0, tiled=False)  13.7 us
    all_gather x1, blocking collectives, shards(): packed_all = lax.all_gather(packed, 'seq', axis=0, tiled=True)  12.4 us
    all_gather x1, blocking collectives, shards(): by_seq = lax.all_gather(over_fsdp, 'seq', axis=0, tiled=False)  11 us
    unnamed x23, local copies, waits for them, and re-layouts  9.48 us
  transfers between devices with their start and end apart: 19, of which 16 were waited for; matrix products, arithmetic and copies ran while one was open for 11% of the time, Pallas kernels for 0%

commit v1 on v0

--- a/solution.py
+++ b/solution.py
@@ -141,7 +141,8 @@
     me_x = ring_x.position()
     ids_col = jnp.broadcast_to(image_ids.astype(jnp.bfloat16)[:, None], (n_rows, width_head))
     packed = jnp.concatenate([heads, grad_out, ids_col], axis=1)
-    packed_all = lax.all_gather(packed, "seq", axis=0, tiled=True)
+    sent = jnp.stack([packed] * lax.axis_size("seq"))
+    packed_all = jnp.concatenate(lax.all_to_all(sent, "seq", 0, 0), axis=0)
     query_all = packed_all[:, :width_head]
     keys_all = packed_all[:, width_head : 2 * width_head]
     values_all = packed_all[:, 2 * width_head : 3 * width_head]

time: 224 us -> 241 us (1.076)
  the two profiles are of different devices: /device:TPU:75 before, /device:TPU:1 now
where the time goes in v1:
time: 241 us; the launch traced here: 239 us
  starting transfers between devices  76.6 us (32%)
  waiting for transfers between devices  53.4 us (22%)
  blocking collectives  43.3 us (18%)
  local copies, waits for them, and re-layouts  27.3 us (11%)
  matrix products  26.6 us (11%)
  other arithmetic  10.8 us (4%)
    ppermute x17, starting transfers between devices, shift(): return lax.ppermute(x, self.axis, perm=pairs)  58.5 us
    ppermute x17, waiting for transfers between devices, shift(): return lax.ppermute(x, self.axis, perm=pairs)  36.4 us
    all_gather x1, blocking collectives, shards(): by_dp = lax.all_gather(over_seq, 'dp', axis=0, tiled=False)  16.3 us
    all_gather x1, blocking collectives, shards(): stack_y = lax.all_gather(w_mine, 'fh', axis=0, tiled=False)  16.3 us
    all_to_all x1, waiting for transfers between devices, shards(): packed_all = jnp.concatenate(lax.all_to_all(sent, 'seq', 0, 0), axis=0)  14.1 us
    ppermute x2, starting transfers between devices, dp_partner(): return lax.ppermute(x, 'dp', perm=pairs)  13.8 us
    unnamed x27, local copies, waits for them, and re-layouts  11.7 us
    all_gather x1, blocking collectives, shards(): by_seq = lax.all_gather(over_fsdp, 'seq', axis=0, tiled=False)  10.7 us
  transfers between devices with their start and end apart: 20, of which 17 were waited for; matrix products, arithmetic and copies ran while one was open for 10% of the time, Pallas kernels for 0%

profile of v1, /device:TPU:1, one launch (start us, length us, event | category | flops | bytes accessed | tf_op | source)
XLA Modules:
  0.0 239.4 jit_solution(11142870628545131331)
XLA Ops:
  1.6 16.3 %all-gather = bf16[768,192]{1,0:T(8,128)(2,1)S(1)} all-gather(bf16[192,192]{1,0:T(8,128)(2,1)S(1)} %constant_dynamic-slice_fusion), channel_id=2, replica_groups=mesh['dp'=4,'seq'=4,'fh'=4,'fz'=8] {'fh'}, dimensions={0}, use_global_device_ids=true | all-gather | bytes 368640 | tf_op jit(solution)/shard_map/all_gather | solution.py:121
  17.9 3.2 %collective-permute-start = (bf16[4,192,192]{2,1,0:T(8,128)(2,1)S(1)}, bf16[4,192,192]{2,1,0:T(8,128)(2,1)}, u32[]{:S(2)}, u32[]{:S(2)}) collective-permute-start(bf16[4,192,192]{2,1,0:T(8,128)(2,1)S(1)} %bitcast.109), channel_id=1, source_target_pairs={{0,1},{1,2},{2,3},{3,4},{4,5},{5,6},{6,7},{7,0},{8,9},{9,10},{10,1... | collective-permute-start | bytes 884744 | tf_op jit(solution)/shard_map/ppermute | solution.py:43
  21.2 8.6 %collective-permute-start.1 = (bf16[4,192,192]{2,1,0:T(8,128)(2,1)S(1)}, bf16[4,192,192]{2,1,0:T(8,128)(2,1)S(1)}, u32[]{:S(2)}, u32[]{:S(2)}) collective-permute-start(bf16[4,192,192]{2,1,0:T(8,128)(2,1)S(1)} %bitcast.110), channel_id=1, source_target_pairs={{0,7},{1,0},{2,1},{3,2},{4,3},{5,4},{6,5},{7,6},{8,15},{9,8},{10,9... | collective-permute-start | bytes 884744 | tf_op jit(solution)/shard_map/ppermute | solution.py:43
  33.1 1.9 collective-permute-start.2
  35.0 1.8 bitcast_dynamic-update-slice_fusion.6
  36.8 4.6 %collective-permute-start.3 = (bf16[4,192,192]{2,1,0:T(8,128)(2,1)S(1)}, bf16[4,192,192]{2,1,0:T(8,128)(2,1)S(1)}, u32[]{:S(2)}, u32[]{:S(2)}) collective-permute-start(bf16[4,192,192]{2,1,0:T(8,128)(2,1)S(1)} %collective-permute-done.1), channel_id=1, source_target_pairs={{0,7},{1,0},{2,1},{3,2},{4,3},{5,4},{6,5},{7,6},{8,15},{9,8},{10,9... | collective-permute-start | bytes 884744 | tf_op jit(solution)/shard_map/ppermute | solution.py:43
  43.0 1.9 collective-permute-start.4
  46.1 5.0 %collective-permute-start.5 = (bf16[4,192,192]{2,1,0:T(8,128)(2,1)S(1)}, bf16[4,192,192]{2,1,0:T(8,128)(2,1)S(1)}, u32[]{:S(2)}, u32[]{:S(2)}) collective-permute-start(bf16[4,192,192]{2,1,0:T(8,128)(2,1)S(1)} %collective-permute-done.3), channel_id=1, source_target_pairs={{0,7},{1,0},{2,1},{3,2},{4,3},{5,4},{6,5},{7,6},{8,15},{9,8},{10,9... | collective-permute-start | bytes 884744 | tf_op jit(solution)/shard_map/ppermute | solution.py:43
  53.0 1.9 collective-permute-start.6
  55.0 1.8 bitcast_dynamic-update-slice_fusion.2
  56.8 4.5 %reshape.146 = bf16[192,4,8,192]{3,2,1,0:T(8,128)(2,1)} reshape(bf16[192,6144]{1,0:T(8,128)(2,1)S(1)} %bitcast.106) | data formatting | bytes 4718592 | tf_op jit(solution)/shard_map/reshape | solution.py:122
  62.1 2.0 collective-permute-done.6
  64.0 1.8 bitcast_dynamic-update-slice_fusion
  65.8 2.6 %gather_fusion.1 = bf16[32,192,192]{2,1,0:T(8,128)(2,1)S(1)} fusion(bf16[32,192,192]{2,1,0:T(8,128)(2,1)} %bitcast.107, s32[1024]{0:T(1024)S(1)} %pad_clamp_fusion), kind=kCustom, calls=%fused_computation.1 | custom fusion | bytes 4718720 | tf_op jit(solution)/shard_map/jit(_take)/gather | solution.py:129
  68.5 2.6 %copy.39 = bf16[6144,192]{0,1:T(8,128)(2,1)} copy(bf16[6144,192]{1,0:T(8,128)(2,1)S(1)} %bitcast.103) | data formatting | bytes 4718592 | tf_op jit(solution)/shard_map/reshape | solution.py:129
  71.1 10.5 %collective-permute-start.7 = (bf16[6144,192]{0,1:T(8,128)(2,1)}, bf16[6144,192]{0,1:T(8,128)(2,1)}, u32[]{:S(2)}, u32[]{:S(2)}) collective-permute-start(bf16[6144,192]{0,1:T(8,128)(2,1)} %copy.39), channel_id=1, source_target_pairs={{0,128},{128,0},{256,384},{384,256},{1,129},{129,1},{257,385},{385... | collective-permute-start | bytes 7077896 | tf_op jit(solution)/shard_map/ppermute | solution.py:22
  81.6 2.6 %convolution_bitcast_fusion.1 = bf16[192,192]{1,0:T(8,128)(2,1)S(1)} fusion(bf16[6144,192]{1,0:T(8,128)(2,1)S(1)} %bitcast.104, bf16[1,192,6144]{2,1,0:T(8,128)(2,1)} %param.5), kind=kOutput, calls=%fused_computation.21 | convolution fusion | flops 452984832 | bytes 4792320 | tf_op jit(solution)/shard_map/dot_general | solution.py:131
  84.2 1.8 collective-permute-done.7
  86.0 2.5 %convolution_bitcast_fusion = bf16[192,192]{1,0:T(8,128)(2,1)S(1)} fusion(bf16[6144,192]{0,1:T(8,128)(2,1)} %collective-permute-done.7, bf16[1,192,6144]{2,1,0:T(8,128)(2,1)S(1)} %copy-done.5), kind=kOutput, calls=%fused_computation.20 | convolution fusion | flops 452984832 | bytes 4792320 | tf_op jit(solution)/shard_map/dot_general | solution.py:132
  89.8 4.2 %all-to-all-start = ((bf16[4,192,640]{2,1,0:T(8,128)(2,1)}), bf16[4,192,640]{2,1,0:T(8,128)(2,1)}, u32[]{:S(2)}, u32[]{:S(2)}) async-start(bf16[4,192,640]{2,1,0:T(8,128)(2,1)} %stack.43), calls=%async_computation | async-start | bytes 1966080 | tf_op jit(solution)/shard_map/all_to_all | solution.py:145
  94.0 14.1 %all-to-all-done = bf16[4,192,640]{2,1,0:T(8,128)(2,1)} async-done(((bf16[4,192,640]{2,1,0:T(8,128)(2,1)}), bf16[4,192,640]{2,1,0:T(8,128)(2,1)}, u32[]{:S(2)}, u32[]{:S(2)}) %all-to-all-start) | async-done | bytes 983072 | tf_op jit(solution)/shard_map/all_to_all | solution.py:145
  116.7 1.8 fusion.13
  118.5 2.9 %multiply_convert_fusion = bf16[768,768]{0,1:T(8,128)(2,1)S(1)} fusion(f32[768,768]{0,1:T(8,128)} %copy-done.6, f32[768]{0:T(1024)S(1)} %fusion.13, f32[768]{0:T(1024)S(1)} %log_add_fusion, bf16[768]{0:T(1024)(128)(2,1)S(1)} %slice_reduce_fusion, bf16[768,640]{1,0:T(8,128)(2,1)} %bitcast.18), kind=kOutput, calls=%fused_computation.16 | convolution fusion | flops 155713536 | bytes 3944448 | tf_op jit(solution)/shard_map/dot_general | solution.py:15
  123.9 4.1 %convert_bitcast_fusion = bf16[8,4,192,192]{2,3,0,1:T(8,128)(2,1)} fusion(bf16[192,4,8,192]{3,2,1,0:T(8,128)(2,1)S(1)} %copy-done.1, pred[]{:T(512)S(6)} %eq.39, bf16[192,128]{1,0:T(8,128)(2,1)S(1)} %convolution_convert_fusion.1, bf16[192,128]{1,0:T(8,128)(2,1)S(1)} %convolution_convert_fusion.2, bf16[192,128]{1,0:T(8,128)(2,1)S(1)} %convolution_convert_fusion), kind=kOutput, calls=%fused_computation.8 | convolution fusion | flops 454496256 | bytes 4866049 | tf_op jit(solution)/shard_map/pyzd,pc->zydc/dot_general | solution.py:177
  128.0 3.4 %collective-permute-start.8 = (bf16[8,4,192,192]{2,3,0,1:T(8,128)(2,1)}, bf16[8,4,192,192]{2,3,0,1:T(8,128)(2,1)}, u32[]{:S(2)}, u32[]{:S(2)}) collective-permute-start(bf16[8,4,192,192]{2,3,0,1:T(8,128)(2,1)} %convert_bitcast_fusion), channel_id=1, source_target_pairs={{0,128},{128,0},{256,384},{384,256},{1,129},{129,1},{257,385},{385... | collective-permute-start | bytes 7077896 | tf_op jit(solution)/shard_map/ppermute | solution.py:22
  133.4 2.4 %fusion.5 = f32[8,4,192,192]{2,3,0,1:T(8,128)S(1)} fusion(bf16[192,4,8,192]{3,2,1,0:T(8,128)(2,1)S(1)} %copy-done.2, pred[]{:T(512)S(6)} %eq.39, bf16[192,128]{1,0:T(8,128)(2,1)S(1)} %convolution_convert_fusion.1, bf16[192,128]{1,0:T(8,128)(2,1)S(1)} %convolution_convert_fusion.2, bf16[192,128]{1,0:T(8,128)(2,1)S(1)} %convolution_convert_fusion), kind=kOutput, calls=%fused_computation.13 | convolution fusion | flops 453316608 | bytes 7225345 | tf_op jit(solution)/shard_map/pyzd,pc->zydc/dot_general | solution.py:179
  136.8 3.0 %convert_add_fusion = f32[8,4,192,192]{2,3,0,1:T(8,128)S(1)} fusion(f32[8,4,192,192]{2,3,0,1:T(8,128)S(1)} %fusion.5, bf16[8,4,192,192]{2,3,0,1:T(8,128)(2,1)} %collective-permute-done.8), kind=kLoop, calls=%fused_computation.4 | loop fusion | flops 2359296 | bytes 11796480 | tf_op jit(solution)/shard_map/add | solution.py:181
  140.0 1.9 collective-permute-start.9
  141.9 4.0 %fusion = bf16[192,6144]{1,0:T(8,128)(2,1)} fusion(f32[192,6144]{1,0:T(8,128)S(1)} %fusion.52, bf16[6144,192]{0,1:T(8,128)(2,1)} %collective-permute-done.7, pred[]{:T(512)S(6)} %eq.39, bf16[192,128]{1,0:T(8,128)(2,1)S(1)} %convolution_convert_fusion.1, bf16[192,128]{1,0:T(8,128)(2,1)S(1)} %convolution_convert_fusion.2, ...), kind=kOutput, calls=%fused_computation.3 | convolution fusion | flops 455675904 | bytes 9584641 | tf_op jit(solution)/shard_map/dot_general | solution.py:15
  145.9 4.5 %collective-permute-start.13 = (bf16[4,192,192]{1,2,0:T(8,128)(2,1)S(1)}, bf16[4,192,192]{1,2,0:T(8,128)(2,1)S(1)}, u32[]{:S(2)}, u32[]{:S(2)}) collective-permute-start(bf16[4,192,192]{1,2,0:T(8,128)(2,1)S(1)} %get-tuple-element.28), channel_id=1, source_target_pairs={{0,7},{1,0},{2,1},{3,2},{4,3},{5,4},{6,5},{7,6},{8,15},{9,8},{10,9... | collective-permute-start | bytes 884744 | tf_op jit(solution)/shard_map/ppermute | solution.py:43
  150.4 3.0 %collective-permute-done.9 = bf16[4,192,192]{1,2,0:T(8,128)(2,1)S(1)} collective-permute-done((bf16[4,192,192]{1,2,0:T(8,128)(2,1)S(1)}, bf16[4,192,192]{1,2,0:T(8,128)(2,1)S(1)}, u32[]{:S(2)}, u32[]{:S(2)}) %collective-permute-start.9) | collective-permute-done | bytes 294944 | tf_op jit(solution)/shard_map/ppermute | solution.py:43
  153.5 1.9 collective-permute-start.10
  155.5 2.7 %collective-permute-done.13 = bf16[4,192,192]{1,2,0:T(8,128)(2,1)S(1)} collective-permute-done((bf16[4,192,192]{1,2,0:T(8,128)(2,1)S(1)}, bf16[4,192,192]{1,2,0:T(8,128)(2,1)S(1)}, u32[]{:S(2)}, u32[]{:S(2)}) %collective-permute-start.13) | collective-permute-done | bytes 294944 | tf_op jit(solution)/shard_map/ppermute | solution.py:43
  158.2 7.9 %collective-permute-done.10 = bf16[4,192,192]{1,2,0:T(8,128)(2,1)S(1)} collective-permute-done((bf16[4,192,192]{1,2,0:T(8,128)(2,1)S(1)}, bf16[4,192,192]{1,2,0:T(8,128)(2,1)S(1)}, u32[]{:S(2)}, u32[]{:S(2)}) %collective-permute-start.10) | collective-permute-done | bytes 294944 | tf_op jit(solution)/shard_map/ppermute | solution.py:43
  166.0 1.6 fusion.17
  167.6 1.9 collective-permute-start.11
  169.5 4.6 %collective-permute-start.14 = (bf16[4,192,192]{1,2,0:T(8,128)(2,1)S(1)}, bf16[4,192,192]{1,2,0:T(8,128)(2,1)S(1)}, u32[]{:S(2)}, u32[]{:S(2)}) collective-permute-start(bf16[4,192,192]{1,2,0:T(8,128)(2,1)S(1)} %get-tuple-element.27), channel_id=1, source_target_pairs={{0,7},{1,0},{2,1},{3,2},{4,3},{5,4},{6,5},{7,6},{8,15},{9,8},{10,9... | collective-permute-start | bytes 884744 | tf_op jit(solution)/shard_map/ppermute | solution.py:43
  174.1 5.0 %collective-permute-done.11 = bf16[4,192,192]{1,2,0:T(8,128)(2,1)S(1)} collective-permute-done((bf16[4,192,192]{1,2,0:T(8,128)(2,1)S(1)}, bf16[4,192,192]{1,2,0:T(8,128)(2,1)S(1)}, u32[]{:S(2)}, u32[]{:S(2)}) %collective-permute-start.11) | collective-permute-done | bytes 294944 | tf_op jit(solution)/shard_map/ppermute | solution.py:43
  180.1 1.6 fusion.16
  181.6 1.9 collective-permute-start.12
  183.6 5.3 %collective-permute-start.15 = (bf16[4,192,192]{1,2,0:T(8,128)(2,1)S(1)}, bf16[4,192,192]{1,2,0:T(8,128)(2,1)S(1)}, u32[]{:S(2)}, u32[]{:S(2)}) collective-permute-start(bf16[4,192,192]{1,2,0:T(8,128)(2,1)S(1)} %get-tuple-element.25), channel_id=1, source_target_pairs={{0,7},{1,0},{2,1},{3,2},{4,3},{5,4},{6,5},{7,6},{8,15},{9,8},{10,9... | collective-permute-start | bytes 884744 | tf_op jit(solution)/shard_map/ppermute | solution.py:43
  189.0 4.1 %collective-permute-done.12 = bf16[4,192,192]{1,2,0:T(8,128)(2,1)S(1)} collective-permute-done((bf16[4,192,192]{1,2,0:T(8,128)(2,1)S(1)}, bf16[4,192,192]{1,2,0:T(8,128)(2,1)S(1)}, u32[]{:S(2)}, u32[]{:S(2)}) %collective-permute-start.12) | collective-permute-done | bytes 294944 | tf_op jit(solution)/shard_map/ppermute | solution.py:43
  195.5 1.9 collective-permute-start.16
  197.5 5.5 %collective-permute-start.18 = (bf16[192,192]{0,1:T(8,128)(2,1)S(1)}, bf16[192,192]{0,1:T(8,128)(2,1)S(1)}, u32[]{:S(2)}, u32[]{:S(2)}) collective-permute-start(bf16[192,192]{0,1:T(8,128)(2,1)S(1)} %get-tuple-element.33), channel_id=1, source_target_pairs={{0,24},{8,0},{16,8},{24,16},{1,25},{9,1},{17,9},{25,17},{2,26},{10... | collective-permute-start | bytes 221192 | tf_op jit(solution)/shard_map/ppermute | solution.py:43
  203.8 1.9 collective-permute-start.17
  205.7 5.5 %collective-permute-done.17 = bf16[192,192]{0,1:T(8,128)(2,1)S(1)} collective-permute-done((bf16[192,192]{0,1:T(8,128)(2,1)S(1)}, bf16[192,192]{0,1:T(8,128)(2,1)S(1)}, u32[]{:S(2)}, u32[]{:S(2)}) %collective-permute-start.17) | collective-permute-done | bytes 73760 | tf_op jit(solution)/shard_map/ppermute | solution.py:43
  211.4 10.7 %all-gather.1 = f32[768,192]{1,0:T(8,128)S(1)} all-gather(f32[192,192]{1,0:T(8,128)S(1)} %copy.47), channel_id=3, replica_groups=mesh['dp'=4,'seq'=4,'fh'=4,'fz'=8] {'seq'}, dimensions={0}, use_global_device_ids=true | all-gather | bytes 737280 | tf_op jit(solution)/shard_map/all_gather | solution.py:184
  222.2 16.3 %all_gather.20 = f32[4,192,192]{2,1,0:T(8,128)S(1)} all-gather(f32[1,192,192]{2,1,0:T(8,128)S(1)} %fusion.28), channel_id=1, replica_groups=mesh['dp'=4,'seq'=4,'fh'=4,'fz'=8] {'dp'}, dimensions={0}, use_global_device_ids=true | all-gather | bytes 737280 | tf_op jit(solution)/shard_map/all_gather | solution.py:188
  (66 shorter events, 30.6 us)
Async XLA Ops:
  0.6 0.9 copy-start
  17.9 15.2 %collective-permute-start = (bf16[4,192,192]{2,1,0:T(8,128)(2,1)S(1)}, bf16[4,192,192]{2,1,0:T(8,128)(2,1)}, u32[]{:S(2)}, u32[]{:S(2)}) collective-permute-start(bf16[4,192,192]{2,1,0:T(8,128)(2,1)S(1)} %bitcast.109), channel_id=1, source_target_pairs={{0,1},{1,2},{2,3},{3,4},{4,5},{5,6},{6,7},{7,0},{8,9},{9,10},{10,1... | collective-permute-start | bytes 884744 | tf_op jit(solution)/shard_map/ppermute | solution.py:43
  21.2 15.6 %collective-permute-start.1 = (bf16[4,192,192]{2,1,0:T(8,128)(2,1)S(1)}, bf16[4,192,192]{2,1,0:T(8,128)(2,1)S(1)}, u32[]{:S(2)}, u32[]{:S(2)}) collective-permute-start(bf16[4,192,192]{2,1,0:T(8,128)(2,1)S(1)} %bitcast.110), channel_id=1, source_target_pairs={{0,7},{1,0},{2,1},{3,2},{4,3},{5,4},{6,5},{7,6},{8,15},{9,8},{10,9... | collective-permute-start | bytes 884744 | tf_op jit(solution)/shard_map/ppermute | solution.py:43
  30.5 26.2 %copy-start.4 = (bf16[1,192,6144]{2,1,0:T(8,128)(2,1)S(1)}, bf16[1,192,6144]{2,1,0:T(8,128)(2,1)}, u32[]{:S(2)}) copy-start(bf16[1,192,6144]{2,1,0:T(8,128)(2,1)} %param.5) | copy-start | bytes 7077892
  33.1 9.9 %collective-permute-start.2 = (bf16[4,192,192]{2,1,0:T(8,128)(2,1)}, bf16[4,192,192]{2,1,0:T(8,128)(2,1)S(1)}, u32[]{:S(2)}, u32[]{:S(2)}) collective-permute-start(bf16[4,192,192]{2,1,0:T(8,128)(2,1)} %collective-permute-done), channel_id=1, source_target_pairs={{0,1},{1,2},{2,3},{3,4},{4,5},{5,6},{6,7},{7,0},{8,9},{9,10},{10,1... | collective-permute-start | bytes 884744 | tf_op jit(solution)/shard_map/ppermute | solution.py:43
  36.8 9.3 %collective-permute-start.3 = (bf16[4,192,192]{2,1,0:T(8,128)(2,1)S(1)}, bf16[4,192,192]{2,1,0:T(8,128)(2,1)S(1)}, u32[]{:S(2)}, u32[]{:S(2)}) collective-permute-start(bf16[4,192,192]{2,1,0:T(8,128)(2,1)S(1)} %collective-permute-done.1), channel_id=1, source_target_pairs={{0,7},{1,0},{2,1},{3,2},{4,3},{5,4},{6,5},{7,6},{8,15},{9,8},{10,9... | collective-permute-start | bytes 884744 | tf_op jit(solution)/shard_map/ppermute | solution.py:43
  43.0 10.0 %collective-permute-start.4 = (bf16[4,192,192]{2,1,0:T(8,128)(2,1)S(1)}, bf16[4,192,192]{2,1,0:T(8,128)(2,1)}, u32[]{:S(2)}, u32[]{:S(2)}) collective-permute-start(bf16[4,192,192]{2,1,0:T(8,128)(2,1)S(1)} %collective-permute-done.2), channel_id=1, source_target_pairs={{0,1},{1,2},{2,3},{3,4},{4,5},{5,6},{6,7},{7,0},{8,9},{9,10},{10,1... | collective-permute-start | bytes 884744 | tf_op jit(solution)/shard_map/ppermute | solution.py:43
  46.1 10.7 %collective-permute-start.5 = (bf16[4,192,192]{2,1,0:T(8,128)(2,1)S(1)}, bf16[4,192,192]{2,1,0:T(8,128)(2,1)S(1)}, u32[]{:S(2)}, u32[]{:S(2)}) collective-permute-start(bf16[4,192,192]{2,1,0:T(8,128)(2,1)S(1)} %collective-permute-done.3), channel_id=1, source_target_pairs={{0,7},{1,0},{2,1},{3,2},{4,3},{5,4},{6,5},{7,6},{8,15},{9,8},{10,9... | collective-permute-start | bytes 884744 | tf_op jit(solution)/shard_map/ppermute | solution.py:43
  53.0 11.0 %collective-permute-start.6 = (bf16[4,192,192]{2,1,0:T(8,128)(2,1)}, bf16[4,192,192]{2,1,0:T(8,128)(2,1)}, u32[]{:S(2)}, u32[]{:S(2)}) collective-permute-start(bf16[4,192,192]{2,1,0:T(8,128)(2,1)} %collective-permute-done.4), channel_id=1, source_target_pairs={{0,1},{1,2},{2,3},{3,4},{4,5},{5,6},{6,7},{7,0},{8,9},{9,10},{10,1... | collective-permute-start | bytes 884744 | tf_op jit(solution)/shard_map/ppermute | solution.py:43
  68.5 13.1 %copy-start.8 = (s32[1,192]{1,0:T(1,128)S(1)}, s32[1,192]{1,0:T(1,128)}, u32[]{:S(2)}) copy-start(s32[1,192]{1,0:T(1,128)} %param.6) | copy-start | bytes 2308
  71.1 14.9 %collective-permute-start.7 = (bf16[6144,192]{0,1:T(8,128)(2,1)}, bf16[6144,192]{0,1:T(8,128)(2,1)}, u32[]{:S(2)}, u32[]{:S(2)}) collective-permute-start(bf16[6144,192]{0,1:T(8,128)(2,1)} %copy.39), channel_id=1, source_target_pairs={{0,128},{128,0},{256,384},{384,256},{1,129},{129,1},{257,385},{385... | collective-permute-start | bytes 7077896 | tf_op jit(solution)/shard_map/ppermute | solution.py:22
  81.6 4.4 %copy-start.5 = (bf16[1,192,6144]{2,1,0:T(8,128)(2,1)S(1)}, bf16[1,192,6144]{2,1,0:T(8,128)(2,1)}, u32[]{:S(2)}) copy-start(bf16[1,192,6144]{2,1,0:T(8,128)(2,1)} %param.5) | copy-start | bytes 7077892
  84.2 4.5 %copy-start.7 = (bf16[1,192,128]{2,1,0:T(8,128)(2,1)S(1)}, bf16[1,192,128]{2,1,0:T(8,128)(2,1)}, u32[]{:S(2)}) copy-start(bf16[1,192,128]{2,1,0:T(8,128)(2,1)} %param.8) | copy-start | bytes 147460
  89.8 18.3 %all-to-all-start = ((bf16[4,192,640]{2,1,0:T(8,128)(2,1)}), bf16[4,192,640]{2,1,0:T(8,128)(2,1)}, u32[]{:S(2)}, u32[]{:S(2)}) async-start(bf16[4,192,640]{2,1,0:T(8,128)(2,1)} %stack.43), calls=%async_computation | async-start | bytes 1966080 | tf_op jit(solution)/shard_map/all_to_all | solution.py:145
  111.7 1.4 copy-start.6
  118.5 5.4 %copy-start.1 = (bf16[192,4,8,192]{3,2,1,0:T(8,128)(2,1)S(1)}, bf16[192,4,8,192]{3,2,1,0:T(8,128)(2,1)}, u32[]{:S(2)}) copy-start(bf16[192,4,8,192]{3,2,1,0:T(8,128)(2,1)} %reshape.146) | copy-start | bytes 7077892
  128.0 8.8 %collective-permute-start.8 = (bf16[8,4,192,192]{2,3,0,1:T(8,128)(2,1)}, bf16[8,4,192,192]{2,3,0,1:T(8,128)(2,1)}, u32[]{:S(2)}, u32[]{:S(2)}) collective-permute-start(bf16[8,4,192,192]{2,3,0,1:T(8,128)(2,1)} %convert_bitcast_fusion), channel_id=1, source_target_pairs={{0,128},{128,0},{256,384},{384,256},{1,129},{129,1},{257,385},{385... | collective-permute-start | bytes 7077896 | tf_op jit(solution)/shard_map/ppermute | solution.py:22
  131.5 1.9 copy-start.2
  139.9 13.5 %copy-start.3 = (f32[8,4,192,192]{2,3,0,1:T(8,128)}, f32[8,4,192,192]{2,3,0,1:T(8,128)S(1)}, u32[]{:S(2)}) copy-start(f32[8,4,192,192]{2,3,0,1:T(8,128)S(1)} %convert_add_fusion) | copy-start | bytes 14155780
  140.0 13.4 %collective-permute-start.9 = (bf16[4,192,192]{1,2,0:T(8,128)(2,1)S(1)}, bf16[4,192,192]{1,2,0:T(8,128)(2,1)S(1)}, u32[]{:S(2)}, u32[]{:S(2)}) collective-permute-start(bf16[4,192,192]{1,2,0:T(8,128)(2,1)S(1)} %get-tuple-element.29), channel_id=1, source_target_pairs={{0,1},{1,2},{2,3},{3,4},{4,5},{5,6},{6,7},{7,0},{8,9},{9,10},{10,1... | collective-permute-start | bytes 884744 | tf_op jit(solution)/shard_map/ppermute | solution.py:43
  145.9 12.3 %collective-permute-start.13 = (bf16[4,192,192]{1,2,0:T(8,128)(2,1)S(1)}, bf16[4,192,192]{1,2,0:T(8,128)(2,1)S(1)}, u32[]{:S(2)}, u32[]{:S(2)}) collective-permute-start(bf16[4,192,192]{1,2,0:T(8,128)(2,1)S(1)} %get-tuple-element.28), channel_id=1, source_target_pairs={{0,7},{1,0},{2,1},{3,2},{4,3},{5,4},{6,5},{7,6},{8,15},{9,8},{10,9... | collective-permute-start | bytes 884744 | tf_op jit(solution)/shard_map/ppermute | solution.py:43
  153.5 12.5 %collective-permute-start.10 = (bf16[4,192,192]{1,2,0:T(8,128)(2,1)S(1)}, bf16[4,192,192]{1,2,0:T(8,128)(2,1)S(1)}, u32[]{:S(2)}, u32[]{:S(2)}) collective-permute-start(bf16[4,192,192]{1,2,0:T(8,128)(2,1)S(1)} %fusion.18), channel_id=1, source_target_pairs={{0,1},{1,2},{2,3},{3,4},{4,5},{5,6},{6,7},{7,0},{8,9},{9,10},{10,1... | collective-permute-start | bytes 884744 | tf_op jit(solution)/shard_map/ppermute | solution.py:43
  167.6 11.6 %collective-permute-start.11 = (bf16[4,192,192]{1,2,0:T(8,128)(2,1)S(1)}, bf16[4,192,192]{1,2,0:T(8,128)(2,1)S(1)}, u32[]{:S(2)}, u32[]{:S(2)}) collective-permute-start(bf16[4,192,192]{1,2,0:T(8,128)(2,1)S(1)} %get-tuple-element.26), channel_id=1, source_target_pairs={{0,1},{1,2},{2,3},{3,4},{4,5},{5,6},{6,7},{7,0},{8,9},{9,10},{10,1... | collective-permute-start | bytes 884744 | tf_op jit(solution)/shard_map/ppermute | solution.py:43
  169.5 10.6 %collective-permute-start.14 = (bf16[4,192,192]{1,2,0:T(8,128)(2,1)S(1)}, bf16[4,192,192]{1,2,0:T(8,128)(2,1)S(1)}, u32[]{:S(2)}, u32[]{:S(2)}) collective-permute-start(bf16[4,192,192]{1,2,0:T(8,128)(2,1)S(1)} %get-tuple-element.27), channel_id=1, source_target_pairs={{0,7},{1,0},{2,1},{3,2},{4,3},{5,4},{6,5},{7,6},{8,15},{9,8},{10,9... | collective-permute-start | bytes 884744 | tf_op jit(solution)/shard_map/ppermute | solution.py:43
  181.6 11.4 %collective-permute-start.12 = (bf16[4,192,192]{1,2,0:T(8,128)(2,1)S(1)}, bf16[4,192,192]{1,2,0:T(8,128)(2,1)S(1)}, u32[]{:S(2)}, u32[]{:S(2)}) collective-permute-start(bf16[4,192,192]{1,2,0:T(8,128)(2,1)S(1)} %get-tuple-element.24), channel_id=1, source_target_pairs={{0,1},{1,2},{2,3},{3,4},{4,5},{5,6},{6,7},{7,0},{8,9},{9,10},{10,1... | collective-permute-start | bytes 884744 | tf_op jit(solution)/shard_map/ppermute | solution.py:43
  183.6 10.7 %collective-permute-start.15 = (bf16[4,192,192]{1,2,0:T(8,128)(2,1)S(1)}, bf16[4,192,192]{1,2,0:T(8,128)(2,1)S(1)}, u32[]{:S(2)}, u32[]{:S(2)}) collective-permute-start(bf16[4,192,192]{1,2,0:T(8,128)(2,1)S(1)} %get-tuple-element.25), channel_id=1, source_target_pairs={{0,7},{1,0},{2,1},{3,2},{4,3},{5,4},{6,5},{7,6},{8,15},{9,8},{10,9... | collective-permute-start | bytes 884744 | tf_op jit(solution)/shard_map/ppermute | solution.py:43
  195.5 8.2 %collective-permute-start.16 = (bf16[192,192]{0,1:T(8,128)(2,1)S(1)}, bf16[192,192]{0,1:T(8,128)(2,1)S(1)}, u32[]{:S(2)}, u32[]{:S(2)}) collective-permute-start(bf16[192,192]{0,1:T(8,128)(2,1)S(1)} %get-tuple-element.32), channel_id=1, source_target_pairs={{0,8},{8,16},{16,24},{24,0},{1,9},{9,17},{17,25},{25,1},{2,10},{10... | collective-permute-start | bytes 221192 | tf_op jit(solution)/shard_map/ppermute | solution.py:43
  197.5 8.2 %collective-permute-start.18 = (bf16[192,192]{0,1:T(8,128)(2,1)S(1)}, bf16[192,192]{0,1:T(8,128)(2,1)S(1)}, u32[]{:S(2)}, u32[]{:S(2)}) collective-permute-start(bf16[192,192]{0,1:T(8,128)(2,1)S(1)} %get-tuple-element.33), channel_id=1, source_target_pairs={{0,24},{8,0},{16,8},{24,16},{1,25},{9,1},{17,9},{25,17},{2,26},{10... | collective-permute-start | bytes 221192 | tf_op jit(solution)/shard_map/ppermute | solution.py:43
  203.8 7.5 %collective-permute-start.17 = (bf16[192,192]{0,1:T(8,128)(2,1)S(1)}, bf16[192,192]{0,1:T(8,128)(2,1)S(1)}, u32[]{:S(2)}, u32[]{:S(2)}) collective-permute-start(bf16[192,192]{0,1:T(8,128)(2,1)S(1)} %fusion.29), channel_id=1, source_target_pairs={{0,8},{8,16},{16,24},{24,0},{1,9},{9,17},{17,25},{25,1},{2,10},{10... | collective-permute-start | bytes 221192 | tf_op jit(solution)/shard_map/ppermute | solution.py:43
